TPU v7x, 256 devices: a whole 4x4x8 slice. The times are simulated.
256 devices in a mesh: seq: 64 (over z, y_lo, x), tp: 4 (over y_hi, core).
Axes of the slice: x: 4, y: 4 (y_hi: 2, y_lo: 2; y = y_hi * 2 + y_lo), z: 8, core: 2. Of those that a mesh axis runs over, the one named last changes fastest.
Arguments:
- tokens: bfloat16 [16384, 2560], P('seq', 'tp'), may hold values from -24 to 24
- norm_gain: bfloat16 [2560], replicated, may hold values from 0.099609375 to 1.8984375
- w_query: bfloat16 [2560, 2560], P(None, 'tp'), may hold values from -0.25 to 0.25
- w_key: bfloat16 [2560, 640], P(None, 'tp'), may hold values from -0.125 to 0.125
- w_value: bfloat16 [2560, 640], P(None, 'tp'), may hold values from -0.125 to 0.125
- w_out: bfloat16 [2560, 2560], P('tp'), may hold values from -0.625 to 0.625
- kv_pool: bfloat16 [1152, 2, 8, 80, 128], P('seq', None, 'tp'), may hold values from -32 to 32
- cache_lengths: int32 [16], replicated, may hold values from 128 to 8192, as said below
- page_table: int32 [16, 72], replicated, may hold values from 0 to 17, as said below
Outputs:
- hidden: bfloat16 [16384, 2560], P('seq', 'tp')
- new_pool: bfloat16 [1152, 2, 8, 80, 128], P('seq', None, 'tp')
Inputs may be any that keep to these rules, and one draw needn't show every extreme that they name: `cache_lengths`: multiples of 128; some group has exactly 8192 and some exactly 128. Group g is the indices g * 4 to g * 4 + 3 of seq. Logical page q of group g (cached or new) lies on member q mod 4 of the group, in local slot page_table[g, q] of that device's 18 slots of kv_pool; for each group and member the 18 logical pages of that member take all 18 slots once.
All inputs are finite; a program needn't handle non-finite values.
Results may differ from a plain program's by a relative error of at most 0.017.
Values may be sent and summed in bfloat16 or wider, within the bound.
No kernel may reach another device: no remote copies, remote signals or barrier semaphores. Data moves between devices by JAX's collectives and lax.ppermute only.
A program may use at most 128 MiB of HBM per device.

v0:
```python
import jax
import jax.numpy as jnp
from jax import lax
from jax.sharding import PartitionSpec as P

HD = 80
PAGE = 128
MAXLEN = 8192
GROUP = 4


norm_eps = 1e-05
rope_base = 1000000.0
masked_score = -1e30


def swapped(x, axis, stride):
    return lax.ppermute(x, axis, [(i, i ^ 1 << stride) for i in range(lax.axis_size(axis))])


def rotate(values, positions):
    head_dim = values.shape[-1]
    half_dim = head_dim // 2
    frequency = rope_base ** (-(jnp.arange(half_dim, dtype=jnp.float32) * 2.0) / head_dim)
    angles = positions.astype(jnp.float32)[:, None] * frequency[None, :]
    cosine = jnp.cos(angles)[:, None, :]
    sine_part = jnp.sin(angles)[:, None, :]
    first_half = values[..., :half_dim]
    second_half = values[..., half_dim:]
    return jnp.concatenate(
        [
            first_half * cosine - second_half * sine_part,
            second_half * cosine + first_half * sine_part,
        ],
        axis=-1,
    )


def attend(state, query, keys, values, valid):
    total_sum, top_score, weight_sum = state
    scale_factor = query.shape[-1] ** (-0.5)
    scores = (
        jnp.einsum("tkgd,pkdn->tkgpn", query, keys, preferred_element_type=jnp.float32)
        * scale_factor
    )
    allowed = valid[:, None, None]
    scores = jnp.where(allowed, scores, masked_score)
    new_top = jnp.maximum(top_score, jnp.max(scores, axis=(3, 4)))
    weights = jnp.where(allowed, jnp.exp(scores - new_top[..., None, None]), 0.0)
    factor = jnp.exp(top_score - new_top)
    weight_sum = weight_sum * factor + jnp.sum(weights, axis=(3, 4))
    total_sum = total_sum * factor[..., None] + jnp.einsum(
        "tkgpn,pkdn->tkgd", weights.astype(jnp.bfloat16), values, preferred_element_type=jnp.float32
    )
    return (total_sum, new_top, weight_sum)


def empty_state(leading, tok_count, kv_heads, group_size, head_dim):
    shape = leading + (tok_count, kv_heads, group_size)
    return (
        jnp.zeros(shape + (head_dim,), jnp.float32),
        jnp.full(shape, masked_score, jnp.float32),
        jnp.zeros(shape, jnp.float32),
    )


def ordered_join(upper_half, mine_now, arrived):
    return jnp.where(
        upper_half,
        jnp.concatenate([arrived, mine_now], axis=0),
        jnp.concatenate([mine_now, arrived], axis=0),
    )


def shards(tokens, norm_gain, w_query, w_key, w_value, w_out, kv_pool, cache_lengths, page_table):
    bit_count = GROUP.bit_length() - 1
    seq_position = lax.axis_index("seq")
    member = seq_position % GROUP
    group_id = seq_position // GROUP
    length = cache_lengths[group_id]
    first_new = length // PAGE
    table_row = page_table[group_id]
    tok_count = tokens.shape[0]
    kv_heads = w_key.shape[1] // HD
    q_heads = w_query.shape[1] // HD
    group_size = q_heads // kv_heads
    tok_pages = tok_count // PAGE
    old_pages = MAXLEN // PAGE
    per_block = min(max(1, 1024 // PAGE), old_pages)
    whole = lax.all_gather(tokens, "tp", axis=1, tiled=True)
    rows_float = whole.astype(jnp.float32)
    normed = (
        rows_float
        * lax.rsqrt(jnp.mean(rows_float * rows_float, axis=-1, keepdims=True) + norm_eps)
        * norm_gain.astype(jnp.float32)
    ).astype(jnp.bfloat16)
    positions = length + member * tok_count + jnp.arange(tok_count, dtype=jnp.int32)
    query_rows = jnp.dot(normed, w_query, preferred_element_type=jnp.float32).reshape(
        tok_count, q_heads, HD
    )
    query = (
        rotate(query_rows, positions)
        .astype(jnp.bfloat16)
        .reshape(tok_count, kv_heads, group_size, HD)
    )
    key_rows = jnp.dot(normed, w_key, preferred_element_type=jnp.float32).reshape(
        tok_count, kv_heads, HD
    )
    new_keys = rotate(key_rows, positions).astype(jnp.bfloat16)
    new_values = (
        jnp.dot(normed, w_value, preferred_element_type=jnp.float32)
        .astype(jnp.bfloat16)
        .reshape(tok_count, kv_heads, HD)
    )
    key_pages = new_keys.reshape(tok_pages, PAGE, kv_heads, HD).transpose(0, 2, 3, 1)
    value_pages = new_values.reshape(tok_pages, PAGE, kv_heads, HD).transpose(0, 2, 3, 1)
    fresh_local = jnp.stack([key_pages, value_pages], axis=1)
    collected = fresh_local[None]
    for bit_pos in range(bit_count):
        arrived = swapped(collected, "seq", bit_pos)
        collected = ordered_join(member >> bit_pos & 1 == 1, collected, arrived)
    pooled = kv_pool[None]
    for bit_pos in range(bit_count):
        arrived = swapped(pooled, "seq", bit_pos)
        pooled = ordered_join(member >> bit_pos & 1 == 1, pooled, arrived)
    pages_dev = kv_pool.shape[0]
    flat_pool = pooled.reshape((GROUP * pages_dev,) + kv_pool.shape[1:])

    def cache_step(step_id, state):
        logical = step_id * per_block + jnp.arange(per_block, dtype=jnp.int32)
        slot_ids = lax.dynamic_slice_in_dim(table_row, step_id * per_block, per_block)
        page_block = jnp.take(flat_pool, logical % GROUP * pages_dev + slot_ids, axis=0)
        valid = (logical < first_new)[None, :, None]
        return attend(state, query, page_block[:, 0], page_block[:, 1], valid)

    step_total = old_pages // per_block
    state = lax.fori_loop(
        0, step_total, cache_step, empty_state((), tok_count, kv_heads, group_size, HD)
    )
    query_pos = member * tok_count + jnp.arange(tok_count, dtype=jnp.int32)[:, None, None]
    page_offsets = (
        jnp.arange(tok_pages, dtype=jnp.int32)[None, :, None] * PAGE
        + jnp.arange(PAGE, dtype=jnp.int32)[None, None, :]
    )
    for source in range(GROUP):
        valid = source * tok_count + page_offsets <= query_pos
        state = attend(state, query, collected[source][:, 0], collected[source][:, 1], valid)
    total_sum, top_score, weight_sum = state
    attended = (
        (total_sum / weight_sum[..., None]).astype(jnp.bfloat16).reshape(tok_count, q_heads * HD)
    )
    out_term = jnp.dot(attended, w_out, preferred_element_type=jnp.float32)
    summed = lax.psum_scatter(
        out_term.astype(jnp.bfloat16), "tp", scatter_dimension=1, tiled=True
    ).astype(jnp.float32)
    hidden = (tokens.astype(jnp.float32) + summed).astype(jnp.bfloat16)
    flat_fresh = collected.reshape((GROUP * tok_pages,) + fresh_local.shape[1:])
    start_offset = (member - first_new) % GROUP
    new_pool = kv_pool
    for page_step in range(tok_pages):
        fresh_index = start_offset + GROUP * page_step
        slot_id = table_row[first_new + fresh_index]
        page_piece = lax.dynamic_index_in_dim(flat_fresh, fresh_index, 0, keepdims=True)
        new_pool = lax.dynamic_update_slice_in_dim(new_pool, page_piece, slot_id, 0)
    return (hidden, new_pool)


def solution(mesh):
    return jax.shard_map(
        shards,
        mesh=mesh,
        in_specs=(
            P("seq", "tp"),
            P(),
            P(None, "tp"),
            P(None, "tp"),
            P(None, "tp"),
            P("tp", None),
            P("seq", None, "tp", None, None),
            P(),
            P(),
        ),
        out_specs=(P("seq", "tp"), P("seq", None, "tp", None, None)),
        check_vma=False,
    )
```

profile of v0, /device:TPU:1, one launch (start us, length us, event | category | flops | bytes accessed | tf_op | source)
XLA Modules:
  0.0 382.1 jit_solution(15098667503905032566)
XLA Ops:
  18.0 25.2 %collective-permute-done = bf16[1,18,2,2,80,128]{5,4,3,2,1,0:T(8,128)(2,1)} collective-permute-done((bf16[1,18,2,2,80,128]{5,4,3,2,1,0:T(8,128)(2,1)}, bf16[1,18,2,2,80,128]{5,4,3,2,1,0:T(8,128)(2,1)}, u32[]{:S(2)}, u32[]{:S(2)}) %collective-permute-start) | collective-permute-done | bytes 1474592 | tf_op jit(solution)/shard_map/ppermute | solution.py:18
  43.2 4.5 %maximum_select_fusion.1 = bf16[2,18,2,2,80,128]{5,4,3,2,1,0:T(8,128)(2,1)} fusion(bf16[1,18,2,2,80,128]{5,4,3,2,1,0:T(8,128)(2,1)} %bitcast.312, bf16[1,18,2,2,80,128]{5,4,3,2,1,0:T(8,128)(2,1)} %collective-permute-done, pred[]{:T(512)S(6)} %eq.20), kind=kLoop, calls=%fused_computation.41 | loop fusion | flops 4423680 | bytes 5898241 | tf_op jit(solution)/shard_map/jit(_where)/select_n | solution.py:68
  64.3 53.9 %collective-permute-done.2 = bf16[1,2,2,2,80,128]{5,4,1,3,2,0:T(8,128)(2,1)S(1)} collective-permute-done((bf16[1,2,2,2,80,128]{5,4,1,3,2,0:T(8,128)(2,1)S(1)}, bf16[1,2,2,2,80,128]{5,4,1,3,2,0:T(8,128)(2,1)S(1)}, u32[]{:S(2)}, u32[]{:S(2)}) %collective-permute-start.2) | collective-permute-done | bytes 163872 | tf_op jit(solution)/shard_map/ppermute | solution.py:18
  120.5 6.2 %collective-permute-done.3 = bf16[2,2,2,2,80,128]{5,4,1,3,2,0:T(8,128)(2,1)S(1)} collective-permute-done((bf16[2,2,2,2,80,128]{5,4,1,3,2,0:T(8,128)(2,1)S(1)}, bf16[2,2,2,2,80,128]{5,4,1,3,2,0:T(8,128)(2,1)S(1)}, u32[]{:S(2)}, u32[]{:S(2)}) %collective-permute-start.3) | collective-permute-done | bytes 327712 | tf_op jit(solution)/shard_map/ppermute | solution.py:18
  134.9 8.0 %maximum_select_fusion = bf16[4,18,2,2,80,128]{5,4,3,2,1,0:T(8,128)(2,1)} fusion(bf16[2,18,2,2,80,128]{5,4,3,2,1,0:T(8,128)(2,1)} %maximum_select_fusion.1, bf16[2,18,2,2,80,128]{5,4,3,2,1,0:T(8,128)(2,1)} %collective-permute-done.1, pred[]{:T(512)S(6)} %eq.19), kind=kLoop, calls=%fused_computation.37 | loop fusion | flops 8847360 | bytes 11796481 | tf_op jit(solution)/shard_map/jit(_where)/select_n | solution.py:68
  143.0 170.9 %while.20 = (s32[]{:T(128)}, f32[256,2,4,80]{0,3,2,1:T(8,128)}, f32[256,2,4]{0,2,1:T(4,128)S(1)}, f32[256,2,4]{0,2,1:T(4,128)S(1)}, s32[]{:T(128)}, /*index=5*/s...) while((s32[]{:T(128)}, f32[256,2,4,80]{0,3,2,1:T(8,128)}, ...), condition=%wide.region_4.5_spmd.clone, body=%wide.region_1.4_spmd.clone.sunk | while | flops 699182208 | bytes 66393996 | solution.py:137
  143.0 4.2 %gather_fusion = bf16[8,2,2,80,128]{4,3,2,1,0:T(8,128)(2,1)} fusion(bf16[72,2,2,80,128]{4,3,2,1,0:T(8,128)(2,1)} %get-tuple-element.399, s32[1024]{0:T(1024)S(1)} %pad_clamp_fusion.2), kind=kCustom, calls=%fused_computation.clone.clone.1 | custom fusion | bytes 1310752 | tf_op jit(solution)/shard_map/while/body/eval_jaxpr/jit(_take)/gather | solution.py:132
  148.4 6.0 %bitcast_reduce_fusion.2 = (f32[256,2,4]{0,2,1:T(4,128)S(1)}, f32[2,8,128,256,4]{3,2,4,1,0:T(8,128)}) fusion(pred[8]{0:T(512)(128)(4,1)S(1)} %get-tuple-element.362, bf16[256,2,4,80]{0,3,2,1:T(8,128)(2,1)} %get-tuple-element.400, bf16[8,2,2,80,128]{4,3,0,2,1:T(8,128)(2,1)S(1)} %copy_select_fusion.2), kind=kOutput, calls=%fused_computation.2.clone.1 | convolution fusion | flops 341833728 | bytes 9052672 | tf_op jit(solution)/shard_map/while/body/eval_jaxpr/tkgd,pkdn->tkgpn/dot_general | solution.py:43
  154.5 4.7 %fusion.111 = f32[256,2,4]{0,2,1:T(4,128)S(1)} fusion(f32[2,8,128,256,4]{3,2,4,1,0:T(8,128)} %get-tuple-element.365, f32[256,2,4]{0,2,1:T(4,128)S(1)} %select_maximum_fusion.2, pred[8]{0:T(512)(128)(4,1)S(1)} %get-tuple-element.362), kind=kLoop, calls=%fused_computation.6.clone.1 | loop fusion | flops 10483712 | bytes 8405000 | tf_op jit(solution)/shard_map/while/body/eval_jaxpr/reduce_sum | solution.py:51
  164.2 4.2 %gather_fusion = bf16[8,2,2,80,128]{4,3,2,1,0:T(8,128)(2,1)} fusion(bf16[72,2,2,80,128]{4,3,2,1,0:T(8,128)(2,1)} %get-tuple-element.399, s32[1024]{0:T(1024)S(1)} %pad_clamp_fusion.2), kind=kCustom, calls=%fused_computation.clone.clone.1 | custom fusion | bytes 1310752 | tf_op jit(solution)/shard_map/while/body/eval_jaxpr/jit(_take)/gather | solution.py:132
  169.6 6.0 %bitcast_reduce_fusion.2 = (f32[256,2,4]{0,2,1:T(4,128)S(1)}, f32[2,8,128,256,4]{3,2,4,1,0:T(8,128)}) fusion(pred[8]{0:T(512)(128)(4,1)S(1)} %get-tuple-element.362, bf16[256,2,4,80]{0,3,2,1:T(8,128)(2,1)} %get-tuple-element.400, bf16[8,2,2,80,128]{4,3,0,2,1:T(8,128)(2,1)S(1)} %copy_select_fusion.2), kind=kOutput, calls=%fused_computation.2.clone.1 | convolution fusion | flops 341833728 | bytes 9052672 | tf_op jit(solution)/shard_map/while/body/eval_jaxpr/tkgd,pkdn->tkgpn/dot_general | solution.py:43
  175.7 4.7 %fusion.111 = f32[256,2,4]{0,2,1:T(4,128)S(1)} fusion(f32[2,8,128,256,4]{3,2,4,1,0:T(8,128)} %get-tuple-element.365, f32[256,2,4]{0,2,1:T(4,128)S(1)} %select_maximum_fusion.2, pred[8]{0:T(512)(128)(4,1)S(1)} %get-tuple-element.362), kind=kLoop, calls=%fused_computation.6.clone.1 | loop fusion | flops 10483712 | bytes 8405000 | tf_op jit(solution)/shard_map/while/body/eval_jaxpr/reduce_sum | solution.py:51
  181.5 4.0 %fusion.113 = f32[256,2,4,80]{0,3,2,1:T(8,128)} fusion(f32[2,8,128,256,4]{3,2,4,1,0:T(8,128)S(1)} %copy-done.1, f32[256,2,4]{0,2,1:T(4,128)S(1)} %select_maximum_fusion.2, pred[8]{0:T(512)(128)(4,1)S(1)} %get-tuple-element.362, f32[256,2,4,80]{0,3,2,1:T(8,128)} %get-tuple-element.382, bf16[8,2,2,80,128]{4,3,0,2,1:T(8,128)(2,1)} %copy-done.2, ...), kind=kOutput, calls=%fused_computation.12.clone.1 | convolution fusion | flops 346521600 | bytes 10044417 | tf_op jit(solution)/shard_map/while/body/eval_jaxpr/tkgpn,pkdn->tkgd/dot_general | solution.py:52
  185.6 4.2 %gather_fusion = bf16[8,2,2,80,128]{4,3,2,1,0:T(8,128)(2,1)} fusion(bf16[72,2,2,80,128]{4,3,2,1,0:T(8,128)(2,1)} %get-tuple-element.399, s32[1024]{0:T(1024)S(1)} %pad_clamp_fusion.2), kind=kCustom, calls=%fused_computation.clone.clone.1 | custom fusion | bytes 1310752 | tf_op jit(solution)/shard_map/while/body/eval_jaxpr/jit(_take)/gather | solution.py:132
  191.0 6.0 %bitcast_reduce_fusion.2 = (f32[256,2,4]{0,2,1:T(4,128)S(1)}, f32[2,8,128,256,4]{3,2,4,1,0:T(8,128)}) fusion(pred[8]{0:T(512)(128)(4,1)S(1)} %get-tuple-element.362, bf16[256,2,4,80]{0,3,2,1:T(8,128)(2,1)} %get-tuple-element.400, bf16[8,2,2,80,128]{4,3,0,2,1:T(8,128)(2,1)S(1)} %copy_select_fusion.2), kind=kOutput, calls=%fused_computation.2.clone.1 | convolution fusion | flops 341833728 | bytes 9052672 | tf_op jit(solution)/shard_map/while/body/eval_jaxpr/tkgd,pkdn->tkgpn/dot_general | solution.py:43
  197.0 4.7 %fusion.111 = f32[256,2,4]{0,2,1:T(4,128)S(1)} fusion(f32[2,8,128,256,4]{3,2,4,1,0:T(8,128)} %get-tuple-element.365, f32[256,2,4]{0,2,1:T(4,128)S(1)} %select_maximum_fusion.2, pred[8]{0:T(512)(128)(4,1)S(1)} %get-tuple-element.362), kind=kLoop, calls=%fused_computation.6.clone.1 | loop fusion | flops 10483712 | bytes 8405000 | tf_op jit(solution)/shard_map/while/body/eval_jaxpr/reduce_sum | solution.py:51
  207.0 4.2 %gather_fusion = bf16[8,2,2,80,128]{4,3,2,1,0:T(8,128)(2,1)} fusion(bf16[72,2,2,80,128]{4,3,2,1,0:T(8,128)(2,1)} %get-tuple-element.399, s32[1024]{0:T(1024)S(1)} %pad_clamp_fusion.2), kind=kCustom, calls=%fused_computation.clone.clone.1 | custom fusion | bytes 1310752 | tf_op jit(solution)/shard_map/while/body/eval_jaxpr/jit(_take)/gather | solution.py:132
  212.4 6.0 %bitcast_reduce_fusion.2 = (f32[256,2,4]{0,2,1:T(4,128)S(1)}, f32[2,8,128,256,4]{3,2,4,1,0:T(8,128)}) fusion(pred[8]{0:T(512)(128)(4,1)S(1)} %get-tuple-element.362, bf16[256,2,4,80]{0,3,2,1:T(8,128)(2,1)} %get-tuple-element.400, bf16[8,2,2,80,128]{4,3,0,2,1:T(8,128)(2,1)S(1)} %copy_select_fusion.2), kind=kOutput, calls=%fused_computation.2.clone.1 | convolution fusion | flops 341833728 | bytes 9052672 | tf_op jit(solution)/shard_map/while/body/eval_jaxpr/tkgd,pkdn->tkgpn/dot_general | solution.py:43
  218.4 4.7 %fusion.111 = f32[256,2,4]{0,2,1:T(4,128)S(1)} fusion(f32[2,8,128,256,4]{3,2,4,1,0:T(8,128)} %get-tuple-element.365, f32[256,2,4]{0,2,1:T(4,128)S(1)} %select_maximum_fusion.2, pred[8]{0:T(512)(128)(4,1)S(1)} %get-tuple-element.362), kind=kLoop, calls=%fused_computation.6.clone.1 | loop fusion | flops 10483712 | bytes 8405000 | tf_op jit(solution)/shard_map/while/body/eval_jaxpr/reduce_sum | solution.py:51
  228.4 4.2 %gather_fusion = bf16[8,2,2,80,128]{4,3,2,1,0:T(8,128)(2,1)} fusion(bf16[72,2,2,80,128]{4,3,2,1,0:T(8,128)(2,1)} %get-tuple-element.399, s32[1024]{0:T(1024)S(1)} %pad_clamp_fusion.2), kind=kCustom, calls=%fused_computation.clone.clone.1 | custom fusion | bytes 1310752 | tf_op jit(solution)/shard_map/while/body/eval_jaxpr/jit(_take)/gather | solution.py:132
  233.8 6.0 %bitcast_reduce_fusion.2 = (f32[256,2,4]{0,2,1:T(4,128)S(1)}, f32[2,8,128,256,4]{3,2,4,1,0:T(8,128)}) fusion(pred[8]{0:T(512)(128)(4,1)S(1)} %get-tuple-element.362, bf16[256,2,4,80]{0,3,2,1:T(8,128)(2,1)} %get-tuple-element.400, bf16[8,2,2,80,128]{4,3,0,2,1:T(8,128)(2,1)S(1)} %copy_select_fusion.2), kind=kOutput, calls=%fused_computation.2.clone.1 | convolution fusion | flops 341833728 | bytes 9052672 | tf_op jit(solution)/shard_map/while/body/eval_jaxpr/tkgd,pkdn->tkgpn/dot_general | solution.py:43
  239.8 4.7 %fusion.111 = f32[256,2,4]{0,2,1:T(4,128)S(1)} fusion(f32[2,8,128,256,4]{3,2,4,1,0:T(8,128)} %get-tuple-element.365, f32[256,2,4]{0,2,1:T(4,128)S(1)} %select_maximum_fusion.2, pred[8]{0:T(512)(128)(4,1)S(1)} %get-tuple-element.362), kind=kLoop, calls=%fused_computation.6.clone.1 | loop fusion | flops 10483712 | bytes 8405000 | tf_op jit(solution)/shard_map/while/body/eval_jaxpr/reduce_sum | solution.py:51
  249.8 4.2 %gather_fusion = bf16[8,2,2,80,128]{4,3,2,1,0:T(8,128)(2,1)} fusion(bf16[72,2,2,80,128]{4,3,2,1,0:T(8,128)(2,1)} %get-tuple-element.399, s32[1024]{0:T(1024)S(1)} %pad_clamp_fusion.2), kind=kCustom, calls=%fused_computation.clone.clone.1 | custom fusion | bytes 1310752 | tf_op jit(solution)/shard_map/while/body/eval_jaxpr/jit(_take)/gather | solution.py:132
  255.1 6.0 %bitcast_reduce_fusion.2 = (f32[256,2,4]{0,2,1:T(4,128)S(1)}, f32[2,8,128,256,4]{3,2,4,1,0:T(8,128)}) fusion(pred[8]{0:T(512)(128)(4,1)S(1)} %get-tuple-element.362, bf16[256,2,4,80]{0,3,2,1:T(8,128)(2,1)} %get-tuple-element.400, bf16[8,2,2,80,128]{4,3,0,2,1:T(8,128)(2,1)S(1)} %copy_select_fusion.2), kind=kOutput, calls=%fused_computation.2.clone.1 | convolution fusion | flops 341833728 | bytes 9052672 | tf_op jit(solution)/shard_map/while/body/eval_jaxpr/tkgd,pkdn->tkgpn/dot_general | solution.py:43
  261.2 4.7 %fusion.111 = f32[256,2,4]{0,2,1:T(4,128)S(1)} fusion(f32[2,8,128,256,4]{3,2,4,1,0:T(8,128)} %get-tuple-element.365, f32[256,2,4]{0,2,1:T(4,128)S(1)} %select_maximum_fusion.2, pred[8]{0:T(512)(128)(4,1)S(1)} %get-tuple-element.362), kind=kLoop, calls=%fused_computation.6.clone.1 | loop fusion | flops 10483712 | bytes 8405000 | tf_op jit(solution)/shard_map/while/body/eval_jaxpr/reduce_sum | solution.py:51
  271.2 4.2 %gather_fusion = bf16[8,2,2,80,128]{4,3,2,1,0:T(8,128)(2,1)} fusion(bf16[72,2,2,80,128]{4,3,2,1,0:T(8,128)(2,1)} %get-tuple-element.399, s32[1024]{0:T(1024)S(1)} %pad_clamp_fusion.2), kind=kCustom, calls=%fused_computation.clone.clone.1 | custom fusion | bytes 1310752 | tf_op jit(solution)/shard_map/while/body/eval_jaxpr/jit(_take)/gather | solution.py:132
  276.5 6.0 %bitcast_reduce_fusion.2 = (f32[256,2,4]{0,2,1:T(4,128)S(1)}, f32[2,8,128,256,4]{3,2,4,1,0:T(8,128)}) fusion(pred[8]{0:T(512)(128)(4,1)S(1)} %get-tuple-element.362, bf16[256,2,4,80]{0,3,2,1:T(8,128)(2,1)} %get-tuple-element.400, bf16[8,2,2,80,128]{4,3,0,2,1:T(8,128)(2,1)S(1)} %copy_select_fusion.2), kind=kOutput, calls=%fused_computation.2.clone.1 | convolution fusion | flops 341833728 | bytes 9052672 | tf_op jit(solution)/shard_map/while/body/eval_jaxpr/tkgd,pkdn->tkgpn/dot_general | solution.py:43
  282.6 4.7 %fusion.111 = f32[256,2,4]{0,2,1:T(4,128)S(1)} fusion(f32[2,8,128,256,4]{3,2,4,1,0:T(8,128)} %get-tuple-element.365, f32[256,2,4]{0,2,1:T(4,128)S(1)} %select_maximum_fusion.2, pred[8]{0:T(512)(128)(4,1)S(1)} %get-tuple-element.362), kind=kLoop, calls=%fused_computation.6.clone.1 | loop fusion | flops 10483712 | bytes 8405000 | tf_op jit(solution)/shard_map/while/body/eval_jaxpr/reduce_sum | solution.py:51
  292.5 4.2 %gather_fusion = bf16[8,2,2,80,128]{4,3,2,1,0:T(8,128)(2,1)} fusion(bf16[72,2,2,80,128]{4,3,2,1,0:T(8,128)(2,1)} %get-tuple-element.399, s32[1024]{0:T(1024)S(1)} %pad_clamp_fusion.2), kind=kCustom, calls=%fused_computation.clone.clone.1 | custom fusion | bytes 1310752 | tf_op jit(solution)/shard_map/while/body/eval_jaxpr/jit(_take)/gather | solution.py:132
  297.9 6.0 %bitcast_reduce_fusion.2 = (f32[256,2,4]{0,2,1:T(4,128)S(1)}, f32[2,8,128,256,4]{3,2,4,1,0:T(8,128)}) fusion(pred[8]{0:T(512)(128)(4,1)S(1)} %get-tuple-element.362, bf16[256,2,4,80]{0,3,2,1:T(8,128)(2,1)} %get-tuple-element.400, bf16[8,2,2,80,128]{4,3,0,2,1:T(8,128)(2,1)S(1)} %copy_select_fusion.2), kind=kOutput, calls=%fused_computation.2.clone.1 | convolution fusion | flops 341833728 | bytes 9052672 | tf_op jit(solution)/shard_map/while/body/eval_jaxpr/tkgd,pkdn->tkgpn/dot_general | solution.py:43
  304.0 4.7 %fusion.111 = f32[256,2,4]{0,2,1:T(4,128)S(1)} fusion(f32[2,8,128,256,4]{3,2,4,1,0:T(8,128)} %get-tuple-element.365, f32[256,2,4]{0,2,1:T(4,128)S(1)} %select_maximum_fusion.2, pred[8]{0:T(512)(128)(4,1)S(1)} %get-tuple-element.362), kind=kLoop, calls=%fused_computation.6.clone.1 | loop fusion | flops 10483712 | bytes 8405000 | tf_op jit(solution)/shard_map/while/body/eval_jaxpr/reduce_sum | solution.py:51
  335.9 35.6 %reduce-scatter.4.cloned.1.call-done = bf16[640,256]{1,0:T(8,128)(2,1)} async-done(((bf16[2560,256]{1,0:T(8,128)(2,1)}), bf16[640,256]{1,0:T(8,128)(2,1)}) %reduce-scatter.4.cloned.1.call-update) | async-done | bytes 327696
  (190 shorter events, 104.2 us)
Async XLA Ops:
  7.2 316.5 %copy-start = (bf16[640,2560]{1,0:T(8,128)(2,1)S(1)}, bf16[640,2560]{1,0:T(8,128)(2,1)}, u32[]{:S(2)}) copy-start(bf16[640,2560]{1,0:T(8,128)(2,1)} %param.16) | copy-start | bytes 9830404
  7.2 8.9 %copy-start.19 = (bf16[2560]{0:T(1024)(128)(2,1)S(1)}, bf16[2560]{0:T(1024)(128)(2,1)}, u32[]{:S(2)}) copy-start(bf16[2560]{0:T(1024)(128)(2,1)} %param.12) | copy-start | bytes 15364
  7.2 5.0 %copy-start.21 = (s32[16]{0:T(128)S(1)}, s32[16]{0:T(128)}, u32[]{:S(2)}) copy-start(s32[16]{0:T(128)} %param.18) | copy-start | bytes 196
  7.2 44.5 %all-gather.2.cloned.1.call-start = ((), (), s32[]{:S(2)}) async-start(), calls=%async_computation.1 | async-start | bytes 1638400 | tf_op jit(solution)/shard_map/all_gather | solution.py:90
  10.0 361.5 %reduce-scatter.4.cloned.1.call-start = ((), (), s32[]{:S(2)}) async-start(), calls=%async_computation.2 | async-start | bytes 1638400
  10.0 33.2 %collective-permute-start = (bf16[1,18,2,2,80,128]{5,4,3,2,1,0:T(8,128)(2,1)}, bf16[1,18,2,2,80,128]{5,4,3,2,1,0:T(8,128)(2,1)}, u32[]{:S(2)}, u32[]{:S(2)}) collective-permute-start(bf16[1,18,2,2,80,128]{5,4,3,2,1,0:T(8,128)(2,1)} %bitcast.311), channel_id=1, source_target_pairs={{0,4},{4,0},{8,12},{12,8},{16,20},{20,16},{24,28},{28,24},{32,36},... | collective-permute-start | bytes 4423688 | tf_op jit(solution)/shard_map/ppermute | solution.py:18
  47.7 87.2 %collective-permute-start.1 = (bf16[2,18,2,2,80,128]{5,4,3,2,1,0:T(8,128)(2,1)}, bf16[2,18,2,2,80,128]{5,4,3,2,1,0:T(8,128)(2,1)}, u32[]{:S(2)}, u32[]{:S(2)}) collective-permute-start(bf16[2,18,2,2,80,128]{5,4,3,2,1,0:T(8,128)(2,1)} %maximum_select_fusion.1), channel_id=1, source_target_pairs={{0,8},{4,12},{8,0},{12,4},{16,24},{20,28},{24,16},{28,20},{32,40},... | collective-permute-start | bytes 8847368 | tf_op jit(solution)/shard_map/ppermute | solution.py:18
  60.1 58.1 %collective-permute-start.2 = (bf16[1,2,2,2,80,128]{5,4,1,3,2,0:T(8,128)(2,1)S(1)}, bf16[1,2,2,2,80,128]{5,4,1,3,2,0:T(8,128)(2,1)S(1)}, u32[]{:S(2)}, u32[]{:S(2)}) collective-permute-start(bf16[1,2,2,2,80,128]{5,4,1,3,2,0:T(8,128)(2,1)S(1)} %maximum_bitcast_fusion), channel_id=1, source_target_pairs={{0,4},{4,0},{8,12},{12,8},{16,20},{20,16},{24,28},{28,24},{32,36},... | collective-permute-start | bytes 491528 | tf_op jit(solution)/shard_map/ppermute | solution.py:18
  118.3 8.5 %collective-permute-start.3 = (bf16[2,2,2,2,80,128]{5,4,1,3,2,0:T(8,128)(2,1)S(1)}, bf16[2,2,2,2,80,128]{5,4,1,3,2,0:T(8,128)(2,1)S(1)}, u32[]{:S(2)}, u32[]{:S(2)}) collective-permute-start(bf16[2,2,2,2,80,128]{5,4,1,3,2,0:T(8,128)(2,1)S(1)} %maximum_select_fusion.3), channel_id=1, source_target_pairs={{0,8},{4,12},{8,0},{12,4},{16,24},{20,28},{24,16},{28,20},{32,40},... | collective-permute-start | bytes 983048 | tf_op jit(solution)/shard_map/ppermute | solution.py:18
  119.7 7.3 %copy-start.9 = (pred[256,2,128]{0,2,1:T(8,128)(4,1)S(1)}, pred[256,2,128]{0,2,1:T(8,128)(4,1)}, u32[]{:S(2)}) copy-start(pred[256,2,128]{0,2,1:T(8,128)(4,1)} %get-tuple-element.278) | copy-start | bytes 196612
  126.9 3.8 copy-start.3
  126.9 3.7 copy-start.12
  126.9 3.7 copy-start.14
  126.9 3.7 copy-start.18
  127.0 5.5 %copy-start.16 = (bf16[2,2,2,80,128]{4,3,0,2,1:T(8,128)(2,1)}, bf16[2,2,2,80,128]{4,3,0,2,1:T(8,128)(2,1)S(1)}, u32[]{:S(2)}) copy-start(bf16[2,2,2,80,128]{4,3,0,2,1:T(8,128)(2,1)S(1)} %get-tuple-element.268) | copy-start | bytes 491524
  127.0 3.7 copy-start.11
  148.4 6.1 %copy-start.2 = (bf16[8,2,2,80,128]{4,3,0,2,1:T(8,128)(2,1)}, bf16[8,2,2,80,128]{4,3,0,2,1:T(8,128)(2,1)S(1)}, u32[]{:S(2)}) copy-start(bf16[8,2,2,80,128]{4,3,0,2,1:T(8,128)(2,1)S(1)} %copy_select_fusion.2) | copy-start | bytes 1966084 | tf_op jit(solution)/shard_map/while
  154.5 5.8 %copy-start.1 = (f32[2,8,128,256,4]{3,2,4,1,0:T(8,128)S(1)}, f32[2,8,128,256,4]{3,2,4,1,0:T(8,128)}, u32[]{:S(2)}) copy-start(f32[2,8,128,256,4]{3,2,4,1,0:T(8,128)} %get-tuple-element.365) | copy-start | bytes 25165828 | tf_op jit(solution)/shard_map/while
  169.6 6.1 %copy-start.2 = (bf16[8,2,2,80,128]{4,3,0,2,1:T(8,128)(2,1)}, bf16[8,2,2,80,128]{4,3,0,2,1:T(8,128)(2,1)S(1)}, u32[]{:S(2)}) copy-start(bf16[8,2,2,80,128]{4,3,0,2,1:T(8,128)(2,1)S(1)} %copy_select_fusion.2) | copy-start | bytes 1966084 | tf_op jit(solution)/shard_map/while
  175.6 5.8 %copy-start.1 = (f32[2,8,128,256,4]{3,2,4,1,0:T(8,128)S(1)}, f32[2,8,128,256,4]{3,2,4,1,0:T(8,128)}, u32[]{:S(2)}) copy-start(f32[2,8,128,256,4]{3,2,4,1,0:T(8,128)} %get-tuple-element.365) | copy-start | bytes 25165828 | tf_op jit(solution)/shard_map/while
  191.0 6.1 %copy-start.2 = (bf16[8,2,2,80,128]{4,3,0,2,1:T(8,128)(2,1)}, bf16[8,2,2,80,128]{4,3,0,2,1:T(8,128)(2,1)S(1)}, u32[]{:S(2)}) copy-start(bf16[8,2,2,80,128]{4,3,0,2,1:T(8,128)(2,1)S(1)} %copy_select_fusion.2) | copy-start | bytes 1966084 | tf_op jit(solution)/shard_map/while
  197.0 5.8 %copy-start.1 = (f32[2,8,128,256,4]{3,2,4,1,0:T(8,128)S(1)}, f32[2,8,128,256,4]{3,2,4,1,0:T(8,128)}, u32[]{:S(2)}) copy-start(f32[2,8,128,256,4]{3,2,4,1,0:T(8,128)} %get-tuple-element.365) | copy-start | bytes 25165828 | tf_op jit(solution)/shard_map/while
  212.4 6.1 %copy-start.2 = (bf16[8,2,2,80,128]{4,3,0,2,1:T(8,128)(2,1)}, bf16[8,2,2,80,128]{4,3,0,2,1:T(8,128)(2,1)S(1)}, u32[]{:S(2)}) copy-start(bf16[8,2,2,80,128]{4,3,0,2,1:T(8,128)(2,1)S(1)} %copy_select_fusion.2) | copy-start | bytes 1966084 | tf_op jit(solution)/shard_map/while
  218.4 5.8 %copy-start.1 = (f32[2,8,128,256,4]{3,2,4,1,0:T(8,128)S(1)}, f32[2,8,128,256,4]{3,2,4,1,0:T(8,128)}, u32[]{:S(2)}) copy-start(f32[2,8,128,256,4]{3,2,4,1,0:T(8,128)} %get-tuple-element.365) | copy-start | bytes 25165828 | tf_op jit(solution)/shard_map/while
  233.7 6.1 %copy-start.2 = (bf16[8,2,2,80,128]{4,3,0,2,1:T(8,128)(2,1)}, bf16[8,2,2,80,128]{4,3,0,2,1:T(8,128)(2,1)S(1)}, u32[]{:S(2)}) copy-start(bf16[8,2,2,80,128]{4,3,0,2,1:T(8,128)(2,1)S(1)} %copy_select_fusion.2) | copy-start | bytes 1966084 | tf_op jit(solution)/shard_map/while
  239.8 5.8 %copy-start.1 = (f32[2,8,128,256,4]{3,2,4,1,0:T(8,128)S(1)}, f32[2,8,128,256,4]{3,2,4,1,0:T(8,128)}, u32[]{:S(2)}) copy-start(f32[2,8,128,256,4]{3,2,4,1,0:T(8,128)} %get-tuple-element.365) | copy-start | bytes 25165828 | tf_op jit(solution)/shard_map/while
  255.1 6.1 %copy-start.2 = (bf16[8,2,2,80,128]{4,3,0,2,1:T(8,128)(2,1)}, bf16[8,2,2,80,128]{4,3,0,2,1:T(8,128)(2,1)S(1)}, u32[]{:S(2)}) copy-start(bf16[8,2,2,80,128]{4,3,0,2,1:T(8,128)(2,1)S(1)} %copy_select_fusion.2) | copy-start | bytes 1966084 | tf_op jit(solution)/shard_map/while
  261.2 5.8 %copy-start.1 = (f32[2,8,128,256,4]{3,2,4,1,0:T(8,128)S(1)}, f32[2,8,128,256,4]{3,2,4,1,0:T(8,128)}, u32[]{:S(2)}) copy-start(f32[2,8,128,256,4]{3,2,4,1,0:T(8,128)} %get-tuple-element.365) | copy-start | bytes 25165828 | tf_op jit(solution)/shard_map/while
  276.5 6.1 %copy-start.2 = (bf16[8,2,2,80,128]{4,3,0,2,1:T(8,128)(2,1)}, bf16[8,2,2,80,128]{4,3,0,2,1:T(8,128)(2,1)S(1)}, u32[]{:S(2)}) copy-start(bf16[8,2,2,80,128]{4,3,0,2,1:T(8,128)(2,1)S(1)} %copy_select_fusion.2) | copy-start | bytes 1966084 | tf_op jit(solution)/shard_map/while
  282.6 5.8 %copy-start.1 = (f32[2,8,128,256,4]{3,2,4,1,0:T(8,128)S(1)}, f32[2,8,128,256,4]{3,2,4,1,0:T(8,128)}, u32[]{:S(2)}) copy-start(f32[2,8,128,256,4]{3,2,4,1,0:T(8,128)} %get-tuple-element.365) | copy-start | bytes 25165828 | tf_op jit(solution)/shard_map/while
  297.9 6.1 %copy-start.2 = (bf16[8,2,2,80,128]{4,3,0,2,1:T(8,128)(2,1)}, bf16[8,2,2,80,128]{4,3,0,2,1:T(8,128)(2,1)S(1)}, u32[]{:S(2)}) copy-start(bf16[8,2,2,80,128]{4,3,0,2,1:T(8,128)(2,1)S(1)} %copy_select_fusion.2) | copy-start | bytes 1966084 | tf_op jit(solution)/shard_map/while
  304.0 5.8 %copy-start.1 = (f32[2,8,128,256,4]{3,2,4,1,0:T(8,128)S(1)}, f32[2,8,128,256,4]{3,2,4,1,0:T(8,128)}, u32[]{:S(2)}) copy-start(f32[2,8,128,256,4]{3,2,4,1,0:T(8,128)} %get-tuple-element.365) | copy-start | bytes 25165828 | tf_op jit(solution)/shard_map/while
  (11 other events, 27.1 us)
Sparse Core Ops, SparseCore 0:
  10.1 28.9 all-gather.1
  328.6 42.8 reduce-scatter.3
where the time goes:
time: 384 us; the launch traced here: 382 us
  waiting for transfers between devices  121 us (32%)
  matrix products  103 us (27%)
  other arithmetic  70.8 us (18%)
  local copies, waits for them, and re-layouts  58 us (15%)
  between operations  21.3 us (6%)
  starting transfers between devices  7.99 us (2%)
    ppermute x4, waiting for transfers between devices, swapped(): lax.ppermute(x, axis, [(i, i ^ 1 << stride) for i in range(lax.axis_size(...  85.4 us
    dot_general x12, matrix products, attend(): jnp.einsum('tkgd,pkdn->tkgpn', query, keys, preferred_element_type=jnp.fl...  56.2 us
    reduce_sum x10, other arithmetic, attend(): weight_sum = weight_sum * factor + jnp.sum(weights, axis=(3, 4))  40.2 us
    dot_general x12, matrix products, attend(): jnp.einsum('tkgpn,pkdn->tkgd', weights.astype(jnp.bfloat16), values, pref...  36.8 us
    unnamed x3, waiting for transfers between devices  35.7 us
    gather x8, local copies, waits for them, and re-layouts, cache_step(): jnp.take(flat_pool, logical % GROUP * pages_dev + slot_ids, axis=0)  33.2 us
    select_n x4, other arithmetic, ordered_join(): jnp.where(upper_half, jnp.concatenate([arrived, mine_now], axis=0), jnp.c...  12.7 us
    select_n x8, other arithmetic, cache_step(): jnp.take(flat_pool, logical % GROUP * pages_dev + slot_ids, axis=0)  9.69 us
  transfers between devices with their start and end apart: 6, of which 4 were waited for; matrix products, arithmetic and copies ran while one was open for 8% of the time, Pallas kernels for 0%

commit v1 on v0

v1 whole, which is shorter than its diff:
```python
import functools

import jax
import jax.numpy as jnp
from jax import lax
from jax.experimental import pallas as pl
from jax.experimental.pallas import tpu as pltpu
from jax.sharding import PartitionSpec as P

HD = 80
PAGE = 128
MAXLEN = 8192
GROUP = 4
PAGES_PER_STEP = 8


norm_eps = 1e-05
rope_base = 1000000.0
masked_score = -1e30


def rotate(values, positions):
    head_dim = values.shape[-1]
    half_dim = head_dim // 2
    frequency = rope_base ** (-(jnp.arange(half_dim, dtype=jnp.float32) * 2.0) / head_dim)
    angles = positions.astype(jnp.float32)[:, None] * frequency[None, :]
    cosine = jnp.cos(angles)[:, None, :]
    sine_part = jnp.sin(angles)[:, None, :]
    first_half = values[..., :half_dim]
    second_half = values[..., half_dim:]
    return jnp.concatenate(
        [
            first_half * cosine - second_half * sine_part,
            second_half * cosine + first_half * sine_part,
        ],
        axis=-1,
    )


def group_shift(x, axis, shift):
    size = lax.axis_size(axis)
    pairs = [(i, i - i % GROUP + (i % GROUP + shift) % GROUP) for i in range(size)]
    return lax.ppermute(x, axis, pairs)


def partial_kernel(
    slots_ref, meta_ref, q_ref, *rest, pages_per_step, cached_steps, rows_per_tok, tok_count, scale
):
    pool_refs = rest[:pages_per_step]
    fresh_ref = rest[pages_per_step]
    o_ref, lse_ref = rest[pages_per_step + 1 : pages_per_step + 3]
    m_sc, l_sc, acc_sc = rest[pages_per_step + 3 :]
    block = pl.program_id(1)
    step = pl.program_id(2)
    cached_count = meta_ref[0]
    member = meta_ref[1]
    source = (member - block + GROUP) % GROUP

    @pl.when(step == 0)
    def _():
        m_sc[...] = jnp.full(m_sc.shape, masked_score, jnp.float32)
        l_sc[...] = jnp.zeros(l_sc.shape, jnp.float32)
        acc_sc[...] = jnp.zeros(acc_sc.shape, jnp.float32)

    def update(kv_pairs, masks):
        q = q_ref[...]
        scores = []
        for (k, _), mask in zip(kv_pairs, masks):
            s = lax.dot_general(q, k, (((1,), (0,)), ((), ())), preferred_element_type=jnp.float32)
            if mask is not None:
                s = jnp.where(mask, s, masked_score)
            scores.append(s)
        m_prev = m_sc[...]
        m_new = m_prev
        for s in scores:
            m_new = jnp.maximum(m_new, jnp.max(s, axis=1, keepdims=True))
        alpha = jnp.exp((m_prev - m_new) * scale)
        l_new = alpha * l_sc[...]
        acc = alpha * acc_sc[...]
        for s, (_, v), mask in zip(scores, kv_pairs, masks):
            p = jnp.exp((s - m_new) * scale)
            if mask is not None:
                p = jnp.where(mask, p, 0.0)
            l_new = l_new + jnp.sum(p, axis=1, keepdims=True)
            acc = acc + lax.dot_general(
                p.astype(jnp.bfloat16), v, (((1,), (1,)), ((), ())), preferred_element_type=jnp.float32
            )
        m_sc[...] = m_new
        l_sc[...] = l_new
        acc_sc[...] = acc

    cached_pairs = [(ref[0], ref[1]) for ref in pool_refs]
    first_page = step * pages_per_step
    is_cached = step < cached_steps

    @pl.when(is_cached & (first_page + pages_per_step <= cached_count))
    def _():
        update(cached_pairs, [None] * pages_per_step)

    @pl.when(is_cached & (first_page < cached_count) & (first_page + pages_per_step > cached_count))
    def _():
        update(cached_pairs, [first_page + i < cached_count for i in range(pages_per_step)])

    fresh_pages = fresh_ref.shape[0]
    fresh_pairs = [(fresh_ref[e, 0], fresh_ref[e, 1]) for e in range(fresh_pages)]
    is_fresh = step == cached_steps

    @pl.when(is_fresh & (source > member))
    def _():
        update(fresh_pairs, [None] * fresh_pages)

    @pl.when(is_fresh & (source == member))
    def _():
        rows = q_ref.shape[0]
        row_tok = lax.broadcasted_iota(jnp.int32, (rows, PAGE), 0) // rows_per_tok
        col = lax.broadcasted_iota(jnp.int32, (rows, PAGE), 1)
        masks = [e * PAGE + col <= row_tok for e in range(fresh_pages)]
        update(fresh_pairs, masks)

    @pl.when(is_fresh)
    def _():
        total = l_sc[...]
        filled = total > 0.0
        safe = jnp.where(filled, total, 1.0)
        o_ref[...] = (acc_sc[...] / safe).astype(o_ref.dtype)
        lse_ref[...] = jnp.where(filled, m_sc[...] * scale + jnp.log(safe), masked_score)


def partial_attention(q_all, kv_pool, fresh, slots, meta, cached_steps):
    blocks, kv_heads, rows, head_dim = q_all.shape
    pages_per_step = PAGES_PER_STEP
    fresh_pages = fresh.shape[0]
    tok_count = fresh_pages * PAGE
    rows_per_tok = rows // tok_count
    scale = head_dim ** (-0.5)

    def pool_map(i):
        def index_map(h, b, j, slots_ref, meta_ref):
            jj = jnp.minimum(j, cached_steps - 1)
            idx = jnp.minimum(jj * pages_per_step + i, jnp.maximum(meta_ref[0] - 1, 0))
            return (slots_ref[idx], 0, h, 0, 0)

        return index_map

    q_spec = pl.BlockSpec((None, None, rows, head_dim), lambda h, b, j, s, m: (b, h, 0, 0))
    pool_specs = [
        pl.BlockSpec((None, 2, None, head_dim, PAGE), pool_map(i)) for i in range(pages_per_step)
    ]
    fresh_spec = pl.BlockSpec(
        (fresh_pages, 2, None, head_dim, PAGE), lambda h, b, j, s, m: (0, 0, h, 0, 0)
    )
    o_spec = pl.BlockSpec((None, None, rows, head_dim), lambda h, b, j, s, m: (b, h, 0, 0))
    lse_spec = pl.BlockSpec((None, None, rows, 1), lambda h, b, j, s, m: (b, h, 0, 0))
    kernel = functools.partial(
        partial_kernel,
        pages_per_step=pages_per_step,
        cached_steps=cached_steps,
        rows_per_tok=rows_per_tok,
        tok_count=tok_count,
        scale=scale,
    )
    keys_per_row = cached_steps * pages_per_step * PAGE + tok_count
    cost = pl.CostEstimate(
        flops=4 * kv_heads * blocks * rows * keys_per_row * head_dim,
        transcendentals=kv_heads * blocks * rows * keys_per_row,
        bytes_accessed=2 * q_all.size * 3 + kv_heads * blocks * keys_per_row * head_dim * 4,
    )
    return pl.pallas_call(
        kernel,
        grid_spec=pltpu.PrefetchScalarGridSpec(
            num_scalar_prefetch=2,
            grid=(kv_heads, blocks, cached_steps + 1),
            in_specs=[q_spec] + pool_specs + [fresh_spec],
            out_specs=[o_spec, lse_spec],
            scratch_shapes=[
                pltpu.VMEM((rows, 1), jnp.float32),
                pltpu.VMEM((rows, 1), jnp.float32),
                pltpu.VMEM((rows, head_dim), jnp.float32),
            ],
        ),
        out_shape=[
            jax.ShapeDtypeStruct((blocks, kv_heads, rows, head_dim), jnp.bfloat16),
            jax.ShapeDtypeStruct((blocks, kv_heads, rows, 1), jnp.float32),
        ],
        compiler_params=pltpu.CompilerParams(
            dimension_semantics=("arbitrary", "arbitrary", "arbitrary")
        ),
        cost_estimate=cost,
    )(slots, meta, q_all, *([kv_pool] * pages_per_step), fresh)


def shards(tokens, norm_gain, w_query, w_key, w_value, w_out, kv_pool, cache_lengths, page_table):
    seq_position = lax.axis_index("seq")
    member = seq_position % GROUP
    group_id = seq_position // GROUP
    length = cache_lengths[group_id]
    first_new = length // PAGE
    table_row = page_table[group_id]
    tok_count = tokens.shape[0]
    kv_heads = w_key.shape[1] // HD
    q_heads = w_query.shape[1] // HD
    group_size = q_heads // kv_heads
    tok_pages = tok_count // PAGE
    cached_per_member = MAXLEN // PAGE // GROUP
    cached_steps = cached_per_member // PAGES_PER_STEP

    whole = lax.all_gather(tokens, "tp", axis=1, tiled=True)
    rows_float = whole.astype(jnp.float32)
    normed = (
        rows_float
        * lax.rsqrt(jnp.mean(rows_float * rows_float, axis=-1, keepdims=True) + norm_eps)
        * norm_gain.astype(jnp.float32)
    ).astype(jnp.bfloat16)
    positions = length + member * tok_count + jnp.arange(tok_count, dtype=jnp.int32)
    query_rows = jnp.dot(normed, w_query, preferred_element_type=jnp.float32).reshape(
        tok_count, q_heads, HD
    )
    query = (
        rotate(query_rows, positions)
        .astype(jnp.bfloat16)
        .reshape(tok_count, kv_heads, group_size, HD)
    )
    key_rows = jnp.dot(normed, w_key, preferred_element_type=jnp.float32).reshape(
        tok_count, kv_heads, HD
    )
    new_keys = rotate(key_rows, positions).astype(jnp.bfloat16)
    new_values = (
        jnp.dot(normed, w_value, preferred_element_type=jnp.float32)
        .astype(jnp.bfloat16)
        .reshape(tok_count, kv_heads, HD)
    )
    key_pages = new_keys.reshape(tok_pages, PAGE, kv_heads, HD).transpose(0, 2, 3, 1)
    value_pages = new_values.reshape(tok_pages, PAGE, kv_heads, HD).transpose(0, 2, 3, 1)
    fresh_local = jnp.stack([key_pages, value_pages], axis=1)

    q_own = query.transpose(1, 0, 2, 3).reshape(kv_heads, tok_count * group_size, HD)
    q_all = jnp.stack([q_own] + [group_shift(q_own, "seq", s) for s in range(1, GROUP)])
    fresh_all = [fresh_local] + [group_shift(fresh_local, "seq", s) for s in range(1, GROUP)]

    slots = table_row[member + GROUP * jnp.arange(cached_per_member, dtype=jnp.int32)]
    cached_count = jnp.maximum((first_new - member + GROUP - 1) // GROUP, 0)
    meta = jnp.stack([cached_count, member]).astype(jnp.int32)
    o_part, lse_part = partial_attention(q_all, kv_pool, fresh_local, slots, meta, cached_steps)

    o_list = [o_part[0]] + [group_shift(o_part[b], "seq", GROUP - b) for b in range(1, GROUP)]
    lse_list = [lse_part[0]] + [group_shift(lse_part[b], "seq", GROUP - b) for b in range(1, GROUP)]
    lse_top = lse_list[0]
    for x in lse_list[1:]:
        lse_top = jnp.maximum(lse_top, x)
    weights = [jnp.exp(x - lse_top) for x in lse_list]
    weight_total = weights[0]
    for w in weights[1:]:
        weight_total = weight_total + w
    combined = weights[0] * o_list[0].astype(jnp.float32)
    for w, o in zip(weights[1:], o_list[1:]):
        combined = combined + w * o.astype(jnp.float32)
    combined = combined / weight_total
    attended = (
        combined.reshape(kv_heads, tok_count, group_size, HD)
        .transpose(1, 0, 2, 3)
        .reshape(tok_count, q_heads * HD)
        .astype(jnp.bfloat16)
    )
    out_term = jnp.dot(attended, w_out, preferred_element_type=jnp.float32)
    summed = lax.psum_scatter(
        out_term.astype(jnp.bfloat16), "tp", scatter_dimension=1, tiled=True
    ).astype(jnp.float32)
    hidden = (tokens.astype(jnp.float32) + summed).astype(jnp.bfloat16)

    fresh_stack = jnp.stack(fresh_all)
    start_offset = (member - first_new) % GROUP
    new_pool = kv_pool
    for extra in range(2):
        page_id = start_offset + GROUP * extra
        source = page_id // tok_pages
        shift_id = (member - source) % GROUP
        page_piece = fresh_stack[shift_id, page_id % tok_pages]
        slot_id = table_row[first_new + page_id]
        new_pool = lax.dynamic_update_slice_in_dim(new_pool, page_piece[None], slot_id, 0)
    return (hidden, new_pool)


def solution(mesh):
    return jax.shard_map(
        shards,
        mesh=mesh,
        in_specs=(
            P("seq", "tp"),
            P(),
            P(None, "tp"),
            P(None, "tp"),
            P(None, "tp"),
            P("tp", None),
            P("seq", None, "tp", None, None),
            P(),
            P(),
        ),
        out_specs=(P("seq", "tp"), P("seq", None, "tp", None, None)),
        check_vma=False,
    )
```

time: 384 us -> 238 us (0.62)
  matrix products: 103 us -> 9.91 us
  Pallas kernels: 0 us -> 67.5 us
  other arithmetic: 70.8 us -> 13.3 us
  local copies, waits for them, and re-layouts: 58 us -> 19.9 us
  waiting for transfers between devices: 121 us -> 90.1 us
  starting transfers between devices: 7.99 us -> 14.2 us
    dot_general x24 -> x0, matrix products: 93 us -> none  [the longest x12 56.2 us: attend(): jnp.einsum('tkgd,pkdn->tkgpn', query, keys, preferred_element_type=jnp.fl...]
    pallas_call x0 -> x1, Pallas kernels: none -> 67.5 us  [partial_attention(): pl.pallas_call(kernel, grid_spec=pltpu.PrefetchScalarGridSpec(num_scalar_...]
    ppermute x4 -> x12, waiting for transfers between devices: 85.4 us -> 45 us  [group_shift(): return lax.ppermute(x, axis, pairs)]
    reduce_sum x10 -> x0, other arithmetic: 40.2 us -> none  [attend(): weight_sum = weight_sum * factor + jnp.sum(weights, axis=(3, 4))]
    gather x8 -> x1, local copies, waits for them, and re-layouts: 33.2 us -> 1.2 us  [shards(): table_row[member + GROUP * jnp.arange(cached_per_member, dtype=jnp.int32)]]
    select_n x12 -> x1, other arithmetic: 22.4 us -> 0.01 us  [shards(): table_row[member + GROUP * jnp.arange(cached_per_member, dtype=jnp.int32)]]
    all_gather x1, waiting for transfers between devices: 0.01 us -> 22.3 us  [shards(): whole = lax.all_gather(tokens, 'tp', axis=1, tiled=True)]
    unnamed x3, waiting for transfers between devices: 35.7 us -> 22.8 us
  transfers between devices with their start and end apart: 6 -> 14, of which waited for: 4 -> 9; matrix products, arithmetic and copies ran while one was open for 8% -> 5% of each run, Pallas kernels for 0% -> 0%
where the time goes in v1:
time: 238 us; the launch traced here: 236 us
  waiting for transfers between devices  90.1 us (38%)
  Pallas kernels  67.5 us (28%)
  between operations  21.6 us (9%)
  local copies, waits for them, and re-layouts  19.9 us (8%)
  starting transfers between devices  14.2 us (6%)
  other arithmetic  13.3 us (6%)
  matrix products  9.91 us (4%)
    pallas_call x1, Pallas kernels, partial_attention(): pl.pallas_call(kernel, grid_spec=pltpu.PrefetchScalarGridSpec(num_scalar_...  67.5 us
    ppermute x12, waiting for transfers between devices, group_shift(): return lax.ppermute(x, axis, pairs)  45 us
    unnamed x3, waiting for transfers between devices  22.8 us
    all_gather x1, waiting for transfers between devices, shards(): whole = lax.all_gather(tokens, 'tp', axis=1, tiled=True)  22.3 us
    ppermute x12, starting transfers between devices, group_shift(): return lax.ppermute(x, axis, pairs)  14.2 us
    unnamed x15, local copies, waits for them, and re-layouts  7.06 us
  transfers between devices with their start and end apart: 14, of which 9 were waited for; matrix products, arithmetic and copies ran while one was open for 5% of the time, Pallas kernels for 0%

profile of v1, /device:TPU:1, one launch (start us, length us, event | category | flops | bytes accessed | tf_op | source)
XLA Modules:
  0.0 236.5 jit_solution(12299264904496067970)
XLA Ops:
  7.2 2.7 %copy.66.rest_0_.rest_1_.rest_2_.rest_3_.rest_4_.rest_5_.rest_6_.rest_7_ = bf16[18,2,2,80,128]{4,3,2,1,0:T(8,128)(2,1)} copy(bf16[18,2,2,80,128]{4,3,2,1,0:T(8,128)(2,1)} %param.15) | data formatting | bytes 2949120
  14.7 1.2 gather_fusion
  16.8 22.3 %all-gather.2.cloned.1.call-done = bf16[256,2560]{1,0:T(8,128)(2,1)} async-done(((bf16[256,640]{1,0:T(8,128)(2,1)}), bf16[256,2560]{1,0:T(8,128)(2,1)}) %all-gather.2.cloned.1.call-update) | async-done | bytes 1310736 | tf_op jit(solution)/shard_map/all_gather | solution.py:207
  39.1 1.7 fusion
  40.8 3.8 %fusion.23 = f32[256,640]{0,1:T(8,128)S(1)} fusion(bf16[2560,640]{1,0:T(8,128)(2,1)} %param.11, bf16[256,2560]{1,0:T(8,128)(2,1)} %all-gather.2.cloned.1.call-done, f32[2560]{0:T(1024)S(1)} %convert_element_type.65, f32[256]{0:T(256)S(1)} %add_rsqrt_fusion), kind=kOutput, calls=%fused_computation.64 | convolution fusion | flops 841482240 | bytes 5254144 | tf_op jit(solution)/shard_map/dot_general | solution.py:215
  45.4 2.0 copy.48
  47.5 1.2 collective-permute-start
  48.7 2.4 %collective-permute-start.1 = (bf16[2,1024,80]{2,1,0:T(8,128)(2,1)}, bf16[2,1024,80]{2,1,0:T(8,128)(2,1)}, u32[]{:S(2)}, u32[]{:S(2)}) collective-permute-start(bf16[2,1024,80]{2,1,0:T(8,128)(2,1)} %bitcast.98), channel_id=1, source_target_pairs={{0,8},{4,12},{8,0},{12,4},{16,24},{20,28},{24,16},{28,20},{32,40},... | collective-permute-start | bytes 983048 | tf_op jit(solution)/shard_map/ppermute | solution.py:43
  51.1 1.2 collective-permute-start.2
  52.2 2.2 fusion.21
  55.9 6.3 %collective-permute-done = bf16[2,1024,80]{2,1,0:T(8,128)(2,1)} collective-permute-done((bf16[2,1024,80]{2,1,0:T(8,128)(2,1)}, bf16[2,1024,80]{2,1,0:T(8,128)(2,1)}, u32[]{:S(2)}, u32[]{:S(2)}) %collective-permute-start) | collective-permute-done | bytes 327712 | tf_op jit(solution)/shard_map/ppermute | solution.py:43
  62.2 12.2 %collective-permute-done.1 = bf16[2,1024,80]{2,1,0:T(8,128)(2,1)} collective-permute-done((bf16[2,1024,80]{2,1,0:T(8,128)(2,1)}, bf16[2,1024,80]{2,1,0:T(8,128)(2,1)}, u32[]{:S(2)}, u32[]{:S(2)}) %collective-permute-start.1) | collective-permute-done | bytes 327712 | tf_op jit(solution)/shard_map/ppermute | solution.py:43
  74.3 3.4 %pad_maximum_fusion.q_ref = bf16[4,2,1024,80]{3,2,1,0:T(8,128)(2,1)} fusion(bf16[1,2,1024,80]{3,2,1,0:T(8,128)(2,1)} %bitcast.13, bf16[1,2,1024,80]{3,2,1,0:T(8,128)(2,1)} %bitcast.12, bf16[1,2,1024,80]{3,2,1,0:T(8,128)(2,1)} %bitcast.11, bf16[1,2,1024,80]{3,2,1,0:T(8,128)(2,1)} %bitcast.100), kind=kLoop, calls=%fused_computation.7 | loop fusion | flops 1966080 | bytes 2621440 | tf_op jit(solution)/shard_map/stack | solution.py:237
  77.8 67.5 %shard_map.104 = (bf16[4,2,1024,80]{3,2,1,0:T(8,128)(2,1)}, f32[4,2,1024,1]{3,2,1,0:T(8,128)}) custom-call(s32[16]{0:T(128)} %gather_fusion, s32[2]{0:T(128)} %pad_add_fusion.meta_ref, bf16[4,2,1024,80]{3,2,1,0:T(8,128)(2,1)} %pad_maximum_fusion.q_ref, bf16[18,2,2,80,128]{4,3,2,1,0:T(8,128)(2,1)} %copy.66.rest_0_.rest_1_.rest_2_.rest_3_.rest_4_.rest_5_.rest_6_.rest_7_, ...), custom_call_target="tpu_custom_call" | custom-call | flops 6039797760 | bytes 9830400 | tf_op jit(solution)/shard_map/pallas_call | solution.py:168
  145.3 3.5 %slice_reduce_fusion.3 = (f32[2,1024]{1,0:T(2,128)S(1)}, f32[2,1024]{1,0:T(2,128)S(1)}, f32[2,1024]{1,0:T(2,128)S(1)}, f32[2,1024]{1,0:T(2,128)S(1)}) fusion(f32[4,2,1024,1]{3,2,1,0:T(8,128)} %get-tuple-element.4), kind=kLoop, calls=%fused_computation.17 | loop fusion | bytes 65536 | tf_op jit(solution)/shard_map/slice | solution.py:246
  150.4 2.5 %collective-permute-start.6 = (bf16[2,1024,80]{2,1,0:T(8,128)(2,1)S(1)}, bf16[2,1024,80]{2,1,0:T(8,128)(2,1)S(1)}, u32[]{:S(2)}, u32[]{:S(2)}) collective-permute-start(bf16[2,1024,80]{2,1,0:T(8,128)(2,1)S(1)} %get-tuple-element.12), channel_id=1, source_target_pairs={{0,12},{4,0},{8,4},{12,8},{16,28},{20,16},{24,20},{28,24},{32,44},... | collective-permute-start | bytes 983048 | tf_op jit(solution)/shard_map/ppermute | solution.py:43
  152.9 1.3 collective-permute-start.7
  155.0 7.6 %collective-permute-done.6 = bf16[2,1024,80]{2,1,0:T(8,128)(2,1)S(1)} collective-permute-done((bf16[2,1024,80]{2,1,0:T(8,128)(2,1)S(1)}, bf16[2,1024,80]{2,1,0:T(8,128)(2,1)S(1)}, u32[]{:S(2)}, u32[]{:S(2)}) %collective-permute-start.6) | collective-permute-done | bytes 327712 | tf_op jit(solution)/shard_map/ppermute | solution.py:43
  162.6 3.4 %collective-permute-done.7 = bf16[2,1024,80]{2,1,0:T(8,128)(2,1)S(1)} collective-permute-done((bf16[2,1024,80]{2,1,0:T(8,128)(2,1)S(1)}, bf16[2,1024,80]{2,1,0:T(8,128)(2,1)S(1)}, u32[]{:S(2)}, u32[]{:S(2)}) %collective-permute-start.7) | collective-permute-done | bytes 327712 | tf_op jit(solution)/shard_map/ppermute | solution.py:43
  166.0 13.6 %collective-permute-done.8 = bf16[2,1024,80]{2,1,0:T(8,128)(2,1)S(1)} collective-permute-done((bf16[2,1024,80]{2,1,0:T(8,128)(2,1)S(1)}, bf16[2,1024,80]{2,1,0:T(8,128)(2,1)S(1)}, u32[]{:S(2)}, u32[]{:S(2)}) %collective-permute-start.8) | collective-permute-done | bytes 327712 | tf_op jit(solution)/shard_map/ppermute | solution.py:43
  179.6 2.5 %fusion.7 = bf16[2,1024,80]{2,1,0:T(8,128)(2,1)} fusion(bf16[2,1024,80]{2,1,0:T(8,128)(2,1)S(1)} %collective-permute-done.8, bf16[2,1024,80]{2,1,0:T(8,128)(2,1)S(1)} %collective-permute-done.7, bf16[2,1024,80]{2,1,0:T(8,128)(2,1)S(1)} %collective-permute-done.6, f32[2,1024]{1,0:T(2,128)S(1)} %get-tuple-element.22, f32[2,1024]{1,0:T(2,128)S(1)} %get-tuple-element.23, ...), kind=kLoop, calls=%fused_computation.18 | loop fusion | flops 2129920 | bytes 1679360 | tf_op jit(solution)/shard_map/convert_element_type | solution.py:262
  182.1 2.0 copy.53
  184.1 3.3 %convolution_convert_fusion = bf16[256,2560]{1,0:T(8,128)(2,1)} fusion(bf16[256,640]{0,1:T(8,128)(2,1)} %bitcast.105, bf16[640,2560]{1,0:T(8,128)(2,1)S(1)} %copy-done), kind=kOutput, calls=%fused_computation.1 | convolution fusion | flops 839516160 | bytes 4915200 | tf_op jit(solution)/shard_map/dot_general | solution.py:264
  187.3 2.4 %copy.55 = bf16[256,2560]{0,1:T(8,128)(2,1)} copy(bf16[256,2560]{1,0:T(8,128)(2,1)} %convolution_convert_fusion) | data formatting | bytes 2621440
  189.9 1.3 collective-permute-start.10
  191.2 2.0 collective-permute-start.11
  193.1 1.4 fusion.26
  198.6 1.7 collective-permute-done.9
  200.6 1.2 pad_maximum_fusion.1
  203.1 22.7 %reduce-scatter.4.cloned.1.call-done = bf16[640,256]{1,0:T(8,128)(2,1)} async-done(((bf16[2560,256]{1,0:T(8,128)(2,1)}), bf16[640,256]{1,0:T(8,128)(2,1)}) %reduce-scatter.4.cloned.1.call-update) | async-done | bytes 327696
  225.9 1.9 copy.56
  227.7 1.9 add_convert_fusion
  (51 shorter events, 8.8 us)
Async XLA Ops:
  7.2 176.9 %copy-start = (bf16[640,2560]{1,0:T(8,128)(2,1)S(1)}, bf16[640,2560]{1,0:T(8,128)(2,1)}, u32[]{:S(2)}) copy-start(bf16[640,2560]{1,0:T(8,128)(2,1)} %param.14) | copy-start | bytes 9830404
  7.2 6.8 %copy-start.3 = (bf16[2560]{0:T(1024)(128)(2,1)S(1)}, bf16[2560]{0:T(1024)(128)(2,1)}, u32[]{:S(2)}) copy-start(bf16[2560]{0:T(1024)(128)(2,1)} %param.10) | copy-start | bytes 15364
  7.2 2.9 %copy-start.5 = (s32[16]{0:T(128)S(1)}, s32[16]{0:T(128)}, u32[]{:S(2)}) copy-start(s32[16]{0:T(128)} %param.16) | copy-start | bytes 196
  7.2 31.9 %all-gather.2.cloned.1.call-start = ((), (), s32[]{:S(2)}) async-start(), calls=%async_computation.1 | async-start | bytes 1638400 | tf_op jit(solution)/shard_map/all_gather | solution.py:207
  10.0 215.9 %reduce-scatter.4.cloned.1.call-start = ((), (), s32[]{:S(2)}) async-start(), calls=%async_computation.2 | async-start | bytes 1638400
  47.5 7.0 %copy-start.2 = (bf16[256,2560]{1,0:T(8,128)(2,1)S(1)}, bf16[256,2560]{1,0:T(8,128)(2,1)}, u32[]{:S(2)}) copy-start(bf16[256,2560]{1,0:T(8,128)(2,1)} %all-gather.2.cloned.1.call-done) | copy-start | bytes 3932164
  47.5 7.0 %copy-start.4 = (bf16[2560,160]{0,1:T(8,128)(2,1)S(1)}, bf16[2560,160]{0,1:T(8,128)(2,1)}, u32[]{:S(2)}) copy-start(bf16[2560,160]{0,1:T(8,128)(2,1)} %param.13) | copy-start | bytes 2457604
  47.5 14.7 %collective-permute-start = (bf16[2,1024,80]{2,1,0:T(8,128)(2,1)}, bf16[2,1024,80]{2,1,0:T(8,128)(2,1)}, u32[]{:S(2)}, u32[]{:S(2)}) collective-permute-start(bf16[2,1024,80]{2,1,0:T(8,128)(2,1)} %bitcast.97), channel_id=1, source_target_pairs={{0,4},{4,8},{8,12},{12,0},{16,20},{20,24},{24,28},{28,16},{32,36},... | collective-permute-start | bytes 983048 | tf_op jit(solution)/shard_map/ppermute | solution.py:43
  48.7 25.7 %collective-permute-start.1 = (bf16[2,1024,80]{2,1,0:T(8,128)(2,1)}, bf16[2,1024,80]{2,1,0:T(8,128)(2,1)}, u32[]{:S(2)}, u32[]{:S(2)}) collective-permute-start(bf16[2,1024,80]{2,1,0:T(8,128)(2,1)} %bitcast.98), channel_id=1, source_target_pairs={{0,8},{4,12},{8,0},{12,4},{16,24},{20,28},{24,16},{28,20},{32,40},... | collective-permute-start | bytes 983048 | tf_op jit(solution)/shard_map/ppermute | solution.py:43
  51.1 23.3 %collective-permute-start.2 = (bf16[2,1024,80]{2,1,0:T(8,128)(2,1)}, bf16[2,1024,80]{2,1,0:T(8,128)(2,1)}, u32[]{:S(2)}, u32[]{:S(2)}) collective-permute-start(bf16[2,1024,80]{2,1,0:T(8,128)(2,1)} %bitcast.99), channel_id=1, source_target_pairs={{0,12},{4,0},{8,4},{12,8},{16,28},{20,16},{24,20},{28,24},{32,44},... | collective-permute-start | bytes 983048 | tf_op jit(solution)/shard_map/ppermute | solution.py:43
  145.3 5.1 %copy-start.1 = (bf16[4,2,1024,80]{3,2,1,0:T(8,128)(2,1)S(1)}, bf16[4,2,1024,80]{3,2,1,0:T(8,128)(2,1)}, u32[]{:S(2)}) copy-start(bf16[4,2,1024,80]{3,2,1,0:T(8,128)(2,1)} %get-tuple-element.5) | copy-start | bytes 3932164
  148.8 5.4 %collective-permute-start.3 = (f32[2,1024,1]{1,0,2:T(2,128)S(1)}, f32[2,1024,1]{1,0,2:T(2,128)S(1)}, u32[]{:S(2)}, u32[]{:S(2)}) collective-permute-start(f32[2,1024,1]{1,0,2:T(2,128)S(1)} %bitcast.110), channel_id=1, source_target_pairs={{0,12},{4,0},{8,4},{12,8},{16,28},{20,16},{24,20},{28,24},{32,44},... | collective-permute-start | bytes 24584 | tf_op jit(solution)/shard_map/ppermute | solution.py:43
  148.9 6.1 %collective-permute-start.4 = (f32[2,1024,1]{1,0,2:T(2,128)S(1)}, f32[2,1024,1]{1,0,2:T(2,128)S(1)}, u32[]{:S(2)}, u32[]{:S(2)}) collective-permute-start(f32[2,1024,1]{1,0,2:T(2,128)S(1)} %bitcast.109), channel_id=1, source_target_pairs={{0,8},{4,12},{8,0},{12,4},{16,24},{20,28},{24,16},{28,20},{32,40},... | collective-permute-start | bytes 24584 | tf_op jit(solution)/shard_map/ppermute | solution.py:43
  149.9 5.0 %collective-permute-start.5 = (f32[2,1024,1]{1,0,2:T(2,128)S(1)}, f32[2,1024,1]{1,0,2:T(2,128)S(1)}, u32[]{:S(2)}, u32[]{:S(2)}) collective-permute-start(f32[2,1024,1]{1,0,2:T(2,128)S(1)} %bitcast.108), channel_id=1, source_target_pairs={{0,4},{4,8},{8,12},{12,0},{16,20},{20,24},{24,28},{28,16},{32,36},... | collective-permute-start | bytes 24584 | tf_op jit(solution)/shard_map/ppermute | solution.py:43
  150.4 12.2 %collective-permute-start.6 = (bf16[2,1024,80]{2,1,0:T(8,128)(2,1)S(1)}, bf16[2,1024,80]{2,1,0:T(8,128)(2,1)S(1)}, u32[]{:S(2)}, u32[]{:S(2)}) collective-permute-start(bf16[2,1024,80]{2,1,0:T(8,128)(2,1)S(1)} %get-tuple-element.12), channel_id=1, source_target_pairs={{0,12},{4,0},{8,4},{12,8},{16,28},{20,16},{24,20},{28,24},{32,44},... | collective-permute-start | bytes 983048 | tf_op jit(solution)/shard_map/ppermute | solution.py:43
  152.9 13.1 %collective-permute-start.7 = (bf16[2,1024,80]{2,1,0:T(8,128)(2,1)S(1)}, bf16[2,1024,80]{2,1,0:T(8,128)(2,1)S(1)}, u32[]{:S(2)}, u32[]{:S(2)}) collective-permute-start(bf16[2,1024,80]{2,1,0:T(8,128)(2,1)S(1)} %get-tuple-element.14), channel_id=1, source_target_pairs={{0,8},{4,12},{8,0},{12,4},{16,24},{20,28},{24,16},{28,20},{32,40},... | collective-permute-start | bytes 983048 | tf_op jit(solution)/shard_map/ppermute | solution.py:43
  154.2 25.4 %collective-permute-start.8 = (bf16[2,1024,80]{2,1,0:T(8,128)(2,1)S(1)}, bf16[2,1024,80]{2,1,0:T(8,128)(2,1)S(1)}, u32[]{:S(2)}, u32[]{:S(2)}) collective-permute-start(bf16[2,1024,80]{2,1,0:T(8,128)(2,1)S(1)} %get-tuple-element.13), channel_id=1, source_target_pairs={{0,4},{4,8},{8,12},{12,0},{16,20},{20,24},{24,28},{28,16},{32,36},... | collective-permute-start | bytes 983048 | tf_op jit(solution)/shard_map/ppermute | solution.py:43
  189.8 10.5 %collective-permute-start.9 = (bf16[2,2,2,80,128]{4,3,2,1,0:T(8,128)(2,1)}, bf16[2,2,2,80,128]{4,3,2,1,0:T(8,128)(2,1)}, u32[]{:S(2)}, u32[]{:S(2)}) collective-permute-start(bf16[2,2,2,80,128]{4,3,2,1,0:T(8,128)(2,1)} %get-tuple-element.20.rest_8_), channel_id=1, source_target_pairs={{0,4},{4,8},{8,12},{12,0},{16,20},{20,24},{24,28},{28,16},{32,36},... | collective-permute-start | bytes 491528 | tf_op jit(solution)/shard_map/ppermute | solution.py:43
  189.9 10.4 %collective-permute-start.10 = (bf16[2,2,2,80,128]{4,3,2,1,0:T(8,128)(2,1)}, bf16[2,2,2,80,128]{4,3,2,1,0:T(8,128)(2,1)}, u32[]{:S(2)}, u32[]{:S(2)}) collective-permute-start(bf16[2,2,2,80,128]{4,3,2,1,0:T(8,128)(2,1)} %get-tuple-element.20.rest_8_), channel_id=1, source_target_pairs={{0,8},{4,12},{8,0},{12,4},{16,24},{20,28},{24,16},{28,20},{32,40},... | collective-permute-start | bytes 491528 | tf_op jit(solution)/shard_map/ppermute | solution.py:43
  191.2 9.4 %collective-permute-start.11 = (bf16[2,2,2,80,128]{4,3,2,1,0:T(8,128)(2,1)}, bf16[2,2,2,80,128]{4,3,2,1,0:T(8,128)(2,1)}, u32[]{:S(2)}, u32[]{:S(2)}) collective-permute-start(bf16[2,2,2,80,128]{4,3,2,1,0:T(8,128)(2,1)} %get-tuple-element.20.rest_8_), channel_id=1, source_target_pairs={{0,12},{4,0},{8,4},{12,8},{16,28},{20,16},{24,20},{28,24},{32,44},... | collective-permute-start | bytes 491528 | tf_op jit(solution)/shard_map/ppermute | solution.py:43
Sparse Core Ops, SparseCore 0:
  10.1 28.9 all-gather.1
  189.9 35.9 reduce-scatter.3
